TPU v7x, 128 devices: a whole 4x4x4 slice. The times are simulated.
128 devices in a mesh: ctx: 16 (over z_lo, y, core), ch: 8 (over z_hi, x).
Axes of the slice: x: 4, y: 4, z: 4 (z_hi: 2, z_lo: 2; z = z_hi * 2 + z_lo), core: 2. Of those that a mesh axis runs over, the one named last changes fastest.
Arguments:
- inputs: bfloat16 [512, 512, 1024], P('ctx', None, 'ch'), may hold values from -600 to 600
- norm_gain: float32 [1024], P('ch'), may hold values from 0.1 to 1.9
- conv_taps: float32 [2, 3, 1024], P(None, None, 'ch'), may hold values from -3 to 3
- factor_one: bfloat16 [512, 512], replicated, may hold values from -0.25 to 0.25
- factor_two: bfloat16 [512, 512], replicated, may hold values from -0.25 to 0.25
- kernel: bfloat16 [512, 512, 1024], P(None, 'ctx', 'ch'), may hold values from -5 to 5
- grad_out: bfloat16 [512, 512, 1024], P('ctx', None, 'ch'), may hold values from -5 to 5
Outputs:
- input_grad: bfloat16 [512, 512, 1024], P('ctx', None, 'ch')
- kernel_grad: bfloat16 [512, 512, 1024], P(None, 'ctx', 'ch')
- factor_one_grad: float32 [512, 512], replicated
- factor_two_grad: float32 [512, 512], replicated
- gain_grad: float32 [1024], P('ch')
- taps_grad: float32 [2, 3, 1024], P(None, None, 'ch')
All inputs are finite; a program needn't handle non-finite values.
Results may differ from a plain program's by a relative error of at most 0.0081.
Values may be sent and summed in bfloat16 or wider, within the bound.
No kernel may reach another device: no remote copies, remote signals or barrier semaphores. Data moves between devices by JAX's collectives and lax.ppermute only.
A program may use at most 192 MiB of HBM per device.

v0:
```python
import math
import jax
import jax.numpy as jnp
from jax import lax
from jax.sharding import PartitionSpec as P

OUTER = 512
INNER = 512
WIDTH = 1024


def shifted(value, axis, steps):
    count = lax.axis_size(axis)
    initial, last = (max(0, -steps), min(count, count - steps))
    return lax.ppermute(value, axis, [(source, source + steps) for source in range(initial, last)])


def on_device(inputs, norm_gain, conv_taps, factor_one, factor_two, kernel, grad_out):
    local_outer, inner, chans = inputs.shape
    rows = local_outer * inner
    taps_count = conv_taps.shape[1]
    flat_in = inputs.reshape(rows, chans).astype(jnp.float32)
    squares = lax.psum(jnp.sum(flat_in * flat_in, axis=1), "ch")
    inverse = lax.rsqrt(squares / WIDTH + 1e-05)
    hat = flat_in * inverse[:, None]
    normed = (hat * norm_gain).astype(jnp.bfloat16)
    earlier = shifted(normed[rows - (taps_count - 1) :], "ctx", 1)
    extended = jnp.concatenate([earlier, normed], 0)
    value_pre = jnp.zeros((rows, chans), jnp.float32)
    gate_pre = jnp.zeros((rows, chans), jnp.float32)
    for offset in range(taps_count):
        window = extended[taps_count - 1 - offset : taps_count - 1 - offset + rows]
        value_pre = value_pre + conv_taps[0, offset] * window
        gate_pre = gate_pre + conv_taps[1, offset] * window
    mixed_in = value_pre.astype(jnp.bfloat16).reshape(local_outer, inner, chans)
    gate = jax.nn.sigmoid(gate_pre)
    cotangent = grad_out.reshape(rows, chans).astype(jnp.float32)
    section_one = jnp.einsum(
        "ijc,jk->ikc", mixed_in, factor_one, preferred_element_type=jnp.float32
    ).astype(jnp.bfloat16)
    out_grad = (cotangent * gate).astype(jnp.bfloat16).reshape(local_outer, inner, chans)
    columns = lax.all_to_all(section_one, "ctx", split_axis=1, concat_axis=0, tiled=True)
    kern = kernel.astype(jnp.float32)
    spectrum = (columns.astype(jnp.float32) * kern).astype(jnp.bfloat16)
    section_two = jnp.einsum(
        "ijc,ik->kjc", spectrum, factor_two, preferred_element_type=jnp.float32
    ).astype(jnp.bfloat16)
    back_rows = lax.all_to_all(section_two, "ctx", split_axis=0, concat_axis=1, tiled=True)
    grad_columns = lax.all_to_all(out_grad, "ctx", split_axis=1, concat_axis=0, tiled=True)
    grad_spec = jnp.einsum(
        "kjc,ik->ijc", grad_columns, factor_two, preferred_element_type=jnp.float32
    )
    kernel_grad = (grad_spec * columns.astype(jnp.float32)).astype(jnp.bfloat16)
    grad_section = (grad_spec * kern).astype(jnp.bfloat16)
    two_part = jnp.einsum("ijc,kjc->ik", spectrum, grad_columns, preferred_element_type=jnp.float32)
    grad_rows = lax.all_to_all(grad_section, "ctx", split_axis=0, concat_axis=1, tiled=True)
    back_flat = back_rows.reshape(rows, chans).astype(jnp.float32)
    grad_gate_pre = cotangent * back_flat * gate * (1.0 - gate)
    grad_mixed = jnp.einsum(
        "ikc,jk->ijc", grad_rows, factor_one, preferred_element_type=jnp.float32
    ).reshape(rows, chans)
    one_part = jnp.einsum("ijc,ikc->jk", mixed_in, grad_rows, preferred_element_type=jnp.float32)
    one_total, two_total = lax.psum((one_part, two_part), ("ctx", "ch"))
    later_value, later_gate = shifted(
        (grad_mixed[: taps_count - 1], grad_gate_pre[: taps_count - 1]), "ctx", -1
    )
    ext_value = jnp.concatenate([grad_mixed, later_value], 0)
    ext_gate = jnp.concatenate([grad_gate_pre, later_gate], 0)
    grad_normed = jnp.zeros((rows, chans), jnp.float32)
    value_taps = []
    gate_taps = []
    for offset in range(taps_count):
        grad_normed = grad_normed + conv_taps[0, offset] * ext_value[offset : offset + rows]
        grad_normed = grad_normed + conv_taps[1, offset] * ext_gate[offset : offset + rows]
        window = extended[taps_count - 1 - offset : taps_count - 1 - offset + rows]
        value_taps.append(jnp.sum(grad_mixed * window, axis=0))
        gate_taps.append(jnp.sum(grad_gate_pre * window, axis=0))
    tap_part = jnp.stack([jnp.stack(value_taps), jnp.stack(gate_taps)])
    gain_part = jnp.sum(grad_normed * hat, axis=0)
    gain_total, taps_total = lax.psum((gain_part, tap_part), "ctx")
    scaled = grad_normed * norm_gain
    row_mean = (
        lax.psum(jnp.sum(scaled * hat, axis=1).astype(jnp.bfloat16), "ch").astype(jnp.float32)
        / WIDTH
    )
    input_grad = (
        (inverse[:, None] * (scaled - hat * row_mean[:, None]))
        .astype(jnp.bfloat16)
        .reshape(local_outer, inner, chans)
    )
    seq_scale = 1.0 / math.sqrt(OUTER * INNER)
    factor_one_grad = one_total / math.sqrt(OUTER * WIDTH)
    factor_two_grad = two_total / math.sqrt(INNER * WIDTH)
    return (
        input_grad,
        kernel_grad,
        factor_one_grad,
        factor_two_grad,
        gain_total * seq_scale,
        taps_total * seq_scale,
    )


def solution(mesh):
    in_specs = (
        P("ctx", None, "ch"),
        P("ch"),
        P(None, None, "ch"),
        P(),
        P(),
        P(None, "ctx", "ch"),
        P("ctx", None, "ch"),
    )
    out_specs = (P("ctx", None, "ch"), P(None, "ctx", "ch"), P(), P(), P("ch"), P(None, None, "ch"))
    return jax.shard_map(
        on_device, mesh=mesh, in_specs=in_specs, out_specs=out_specs, check_vma=False
    )
```

profile of v0, /device:TPU:1, one launch (start us, length us, event | category | flops | bytes accessed | tf_op | source)
XLA Modules:
  0.0 595.7 jit_solution(9241242994487293887)
XLA Ops:
  7.2 6.5 %copy.43 = bf16[32,512,128]{1,2,0:T(8,128)(2,1)} copy(bf16[32,512,128]{2,1,0:T(8,128)(2,1)} %param.7) | data formatting | bytes 8388608 | tf_op args[0]
  13.7 3.1 multiply_reduce_fusion.3
  17.5 7.1 %copy.44 = f32[32,512,128]{2,1,0:T(8,128)} copy(bf16[32,512,128]{1,2,0:T(8,128)(2,1)} %copy.43) | data formatting | bytes 12582912 | tf_op jit(solution)/shard_map/convert_element_type | solution.py:22
  24.6 75.1 %all-reduce.5.cloned.1.call-done = f32[16384]{0:T(1024)} async-done(((f32[16384]{0:T(1024)}), f32[16384]{0:T(1024)}) %all-reduce.5.cloned.1.call-update) | async-done | bytes 65552 | tf_op jit(solution)/shard_map/psum | solution.py:23
  100.7 5.5 multiply_convert_fusion.2
  106.2 9.4 %collective-permute-start = (bf16[2,128]{1,0:T(2,128)(2,1)S(1)}, bf16[2,128]{1,0:T(2,128)(2,1)S(1)}, u32[]{:S(2)}, u32[]{:S(2)}) collective-permute-start(bf16[2,128]{1,0:T(2,128)(2,1)S(1)} %slice.68), channel_id=1, source_target_pairs={{0,8},{8,16},{16,24},{24,32},{32,40},{40,48},{48,56},{56,64},{64,7... | collective-permute-start | bytes 1544 | tf_op jit(solution)/shard_map/ppermute | solution.py:15
  116.3 6.5 %fusion.10 = (bf16[16384,128]{1,0:T(8,128)(2,1)}, bf16[16384,128]{1,0:T(8,128)(2,1)S(1)}) fusion(bf16[32,512,128]{2,1,0:T(8,128)(2,1)S(1)} %copy-done.9, bf16[16384,128]{1,0:T(8,128)(2,1)S(1)} %multiply_convert_fusion.2, bf16[2,128]{1,0:T(2,128)(2,1)S(1)} %collective-permute-done, f32[128]{0:T(128)S(1)} %get-tuple-element.44, f32[128]{0:T(128)S(1)} %get-tuple-element.45, ...), kind=kLoop, calls=%fused_computation.29 | loop fusion | flops 44040192 | bytes 16779264 | tf_op jit(solution)/shard_map/convert_element_type | solution.py:41
  122.8 3.0 fusion.21
  125.9 1.9 copy-done.7
  127.8 4.4 convert_bitcast_fusion.3
  132.2 7.9 %copy.55 = bf16[32,512,128]{2,0,1:T(8,128)(2,1)} copy(bf16[32,512,128]{1,2,0:T(8,128)(2,1)} %convert_bitcast_fusion.3) | data formatting | bytes 8388608 | tf_op jit(solution)/shard_map/convert_element_type | solution.py:40
  140.1 5.6 all-to-all-start.2
  145.6 6.9 %copy.45 = bf16[32,512,128]{2,0,1:T(8,128)(2,1)} copy(bf16[32,512,128]{2,1,0:T(8,128)(2,1)} %bitcast.103) | data formatting | bytes 8388608 | tf_op jit(solution)/shard_map/reshape | solution.py:41
  152.6 48.9 %all-to-all-done.2 = bf16[32,512,128]{2,0,1:T(8,128)(2,1)} async-done(((bf16[32,512,128]{2,0,1:T(8,128)(2,1)}), bf16[32,512,128]{2,0,1:T(8,128)(2,1)}, u32[]{:S(2)}, u32[]{:S(2)}) %all-to-all-start.2) | async-done | bytes 4194336 | tf_op jit(solution)/shard_map/all_to_all | solution.py:42
  201.5 5.5 all-to-all-start
  207.0 7.6 %copy.49 = bf16[512,32,128]{0,2,1:T(8,128)(2,1)} copy(bf16[512,32,128]{2,1,0:T(8,128)(2,1)} %param.12) | data formatting | bytes 8388608 | tf_op args[5]
  214.5 3.8 copy.56
  219.5 4.2 copy.57
  223.8 9.9 %copy.58 = f32[512,32,128]{0,2,1:T(8,128)} copy(f32[512,32,128]{2,1,0:T(8,128)} %bitcast.102) | data formatting | bytes 16777216 | tf_op jit(solution)/shard_map/convert_element_type | solution.py:44
  233.7 8.9 %convert_bitcast_fusion.2 = bf16[512,32,128]{0,2,1:T(8,128)(2,1)} fusion(bf16[512,512]{1,0:T(8,128)(2,1)S(1)} %copy-done, f32[512,32,128]{0,2,1:T(8,128)} %copy.58, bf16[512,32,128]{0,2,1:T(8,128)(2,1)} %copy.49), kind=kOutput, calls=%fused_computation.66 | convolution fusion | flops 2155872256 | bytes 17301504 | tf_op jit(solution)/shard_map/ijc,ik->kjc/dot_general | solution.py:45
  242.6 7.9 %copy.59 = bf16[512,32,128]{2,1,0:T(8,128)(2,1)} copy(bf16[512,32,128]{0,2,1:T(8,128)(2,1)} %convert_bitcast_fusion.2) | data formatting | bytes 8388608 | tf_op jit(solution)/shard_map/convert_element_type | solution.py:47
  250.6 11.9 %all-to-all-done = bf16[32,512,128]{2,0,1:T(8,128)(2,1)} async-done(((bf16[32,512,128]{2,0,1:T(8,128)(2,1)}), bf16[32,512,128]{2,0,1:T(8,128)(2,1)}, u32[]{:S(2)}, u32[]{:S(2)}) %all-to-all-start) | async-done | bytes 4194336 | tf_op jit(solution)/shard_map/all_to_all | solution.py:49
  262.5 5.1 all-to-all-start.3
  267.6 4.1 copy.47
  271.7 12.6 %fusion.29 = (bf16[512,32,128]{0,2,1:T(8,128)(2,1)}, bf16[512,32,128]{0,2,1:T(8,128)(2,1)}) fusion(f32[512,32,128]{0,2,1:T(8,128)} %copy.58, bf16[512,32,128]{0,2,1:T(8,128)(2,1)S(1)} %copy-done.2, bf16[512,512]{1,0:T(8,128)(2,1)S(1)} %copy-done, bf16[512,32,128]{2,1,0:T(8,128)(2,1)S(1)} %bitcast.100), kind=kOutput, calls=%fused_computation.53 | convolution fusion | flops 2157969408 | bytes 25690112 | tf_op jit(solution)/shard_map/kjc,ik->ijc/dot_general | solution.py:50
  284.4 7.9 %copy.50 = bf16[512,32,128]{2,1,0:T(8,128)(2,1)} copy(bf16[512,32,128]{0,2,1:T(8,128)(2,1)} %get-tuple-element.42) | data formatting | bytes 8388608 | tf_op jit(solution)/shard_map/convert_element_type | solution.py:54
  292.3 31.2 %all-to-all-done.3 = bf16[512,32,128]{2,1,0:T(8,128)(2,1)} async-done(((bf16[512,32,128]{2,1,0:T(8,128)(2,1)}), bf16[512,32,128]{2,1,0:T(8,128)(2,1)}, u32[]{:S(2)}, u32[]{:S(2)}) %all-to-all-start.3) | async-done | bytes 4194336 | tf_op jit(solution)/shard_map/all_to_all | solution.py:48
  323.4 5.0 all-to-all-start.1
  328.5 7.8 %copy.64 = bf16[512,32,128]{2,1,0:T(8,128)(2,1)} copy(bf16[512,32,128]{0,2,1:T(8,128)(2,1)} %get-tuple-element.41) | data formatting | bytes 8388608
  336.4 11.0 %fusion.35 = f32[512,512]{1,0:T(8,128)} fusion(bf16[512,32,128]{2,1,0:T(8,128)(2,1)} %bitcast.101, f32[512,32,128]{0,2,1:T(8,128)} %copy.58, bf16[512,32,128]{0,2,1:T(8,128)(2,1)} %copy.49), kind=kOutput, calls=%fused_computation.73 | convolution fusion | flops 2153775104 | bytes 17825792 | tf_op jit(solution)/shard_map/ijc,kjc->ik/dot_general | solution.py:55
  347.4 3.4 convert_bitcast_fusion
  350.8 4.3 copy.60
  355.1 29.1 %all-to-all-done.1 = bf16[512,32,128]{2,1,0:T(8,128)(2,1)} async-done(((bf16[512,32,128]{2,1,0:T(8,128)(2,1)}), bf16[512,32,128]{2,1,0:T(8,128)(2,1)}, u32[]{:S(2)}, u32[]{:S(2)}) %all-to-all-start.1) | async-done | bytes 4194336 | tf_op jit(solution)/shard_map/all_to_all | solution.py:56
  384.2 3.6 copy.51
  387.8 1.9 copy-done.10
  389.7 3.3 convolution_bitcast_fusion.1
  393.1 10.3 %multiply_reduce_fusion = (f32[128]{0:T(128)S(1)}, f32[32,512,128]{1,2,0:T(8,128)}) fusion(f32[128]{0:T(128)S(1)} %copy-done.12, f32[32,512]{1,0:T(8,128)S(1)} %mul.250, bf16[32,512,128]{1,2,0:T(8,128)(2,1)} %copy.43, bf16[32,512,128]{2,1,0:T(8,128)(2,1)} %bitcast.108, bf16[512,512]{1,0:T(8,128)(2,1)S(1)} %copy-done.11), kind=kOutput, calls=%fused_computation.55 | convolution fusion | flops 2162163712 | bytes 17368064 | tf_op jit(solution)/shard_map/ikc,jk->ijc/dot_general | solution.py:59
  403.4 8.9 %copy.53 = f32[32,512,128]{2,1,0:T(8,128)} copy(f32[32,512,128]{1,2,0:T(8,128)} %get-tuple-element.50) | data formatting | bytes 16777216 | tf_op jit(solution)/shard_map/ikc,jk->ijc/transpose | solution.py:59
  413.0 14.0 %fusion.22 = (f32[128]{0:T(128)S(1)}, f32[128]{0:T(128)S(1)}, f32[128]{0:T(128)S(1)}, f32[128]{0:T(128)S(1)}, f32[128]{0:T(128)S(1)}, /*index=5*/f32[16384,128]{1,0:T(8,128)S(1)}) fusion(bf16[16384,128]{1,0:T(8,128)(2,1)} %copy-done.3, bf16[2,128]{1,0:T(2,128)(2,1)S(1)} %collective-permute-done, bf16[16384,128]{1,0:T(8,128)(2,1)} %copy-done.5, ...), kind=kLoop, calls=%fused_computation.41 | loop fusion | flops 60816768 | bytes 37753344 | tf_op jit(solution)/shard_map/reduce_sum | solution.py:77
  427.0 3.3 copy-done.6
  430.3 2.6 collective-permute-start.2
  436.2 1.9 collective-permute-done.1
  438.1 31.9 %multiply_reduce_fusion.1 = (f32[128]{0:T(128)S(1)}, bf16[16384]{0:T(1024)(128)(2,1)S(1)}, f32[16384,128]{1,0:T(8,128)}) fusion(f32[32,512,128]{2,1,0:T(8,128)} %copy.44, f32[16384]{0:T(1024)S(1)} %add_rsqrt_fusion, f32[128]{0:T(128)S(1)} %copy-done.12, f32[2,128]{1,0:T(2,128)S(1)} %collective-permute-done.2, f32[16384,128]{1,0:T(8,128)} %copy-done.6, ...), kind=kLoop, calls=%fused_computation.57 | loop fusion | flops 44023680 | bytes 33658880 | tf_op jit(solution)/shard_map/reduce_sum | solution.py:79
  470.1 31.7 %psum.43 = bf16[16384]{0:T(1024)(128)(2,1)S(1)} all-reduce(bf16[16384]{0:T(1024)(128)(2,1)S(1)} %get-tuple-element.25), channel_id=1, replica_groups=mesh['ctx'=16,'ch'=8] {'ch'}, use_global_device_ids=true, to_apply=%region_3.0 | all-reduce | flops 16384 | bytes 65536 | tf_op jit(solution)/shard_map/psum | solution.py:83
  501.8 11.5 %multiply_convert_fusion.1 = bf16[16384,128]{1,0:T(8,128)(2,1)} fusion(f32[16384,128]{1,0:T(8,128)} %get-tuple-element.38, f32[32,512,128]{2,1,0:T(8,128)} %copy.44, f32[16384]{0:T(1024)S(1)} %convert_multiply_fusion.15, f32[128]{0:T(128)S(1)} %copy-done.12, f32[16384]{0:T(1024)S(1)} %add_rsqrt_fusion), kind=kLoop, calls=%fused_computation.58 | loop fusion | flops 12582912 | bytes 21103104 | tf_op jit(solution)/shard_map/convert_element_type | solution.py:88
  513.3 31.7 %all-reduce.1 = (f32[128]{0:T(128)S(1)}, f32[2,3,128]{2,1,0:T(4,128)S(1)}) all-reduce(f32[128]{0:T(128)S(1)} %get-tuple-element.24, f32[2,3,128]{2,1,0:T(4,128)S(1)} %pad_maximum_fusion.3), channel_id=1, replica_groups=mesh['ctx'=16,'ch'=8] {'ctx'}, use_global_device_ids=true, to_apply=%region_7.0 | all-reduce | flops 896 | bytes 7168 | tf_op jit(solution)/shard_map/psum | solution.py:80
  546.2 39.4 %all-reduce.7.cloned.1.call-done = (f32[512,512]{1,0:T(8,128)}, f32[512,512]{1,0:T(8,128)}) async-done(((f32[512,512]{1,0:T(8,128)}, f32[512,512]{1,0:T(8,128)}), (f32[512,512]{1,0:T(8,128)}, f32[512,512]{1,0:T(8,128)})) %all-reduce.7.cloned.1.call-update) | async-done | bytes 2097168 | tf_op jit(solution)/shard_map/psum | solution.py:63
  585.5 3.1 broadcast_multiply_fusion
  (46 shorter events, 8.8 us)
Async XLA Ops:
  7.2 226.5 %copy-start = (bf16[512,512]{1,0:T(8,128)(2,1)S(1)}, bf16[512,512]{1,0:T(8,128)(2,1)}, u32[]{:S(2)}) copy-start(bf16[512,512]{1,0:T(8,128)(2,1)} %param.11) | copy-start | bytes 1572868
  7.2 92.5 %all-reduce.5.cloned.1.call-start = ((), (), s32[]{:S(2)}) async-start(), calls=%async_computation.4 | async-start | bytes 131072 | tf_op jit(solution)/shard_map/psum | solution.py:23
  13.7 87.0 %copy-start.12 = (f32[128]{0:T(128)S(1)}, f32[128]{0:T(128)}, u32[]{:S(2)}) copy-start(f32[128]{0:T(128)} %param.8) | copy-start | bytes 1540
  24.6 91.1 %copy-start.13 = (f32[2,3,128]{2,0,1:T(2,128)S(1)}, f32[2,3,128]{2,0,1:T(2,128)}, u32[]{:S(2)}) copy-start(f32[2,3,128]{2,0,1:T(2,128)} %param.9) | copy-start | bytes 9220
  99.7 16.6 %copy-start.9 = (bf16[32,512,128]{2,1,0:T(8,128)(2,1)S(1)}, bf16[32,512,128]{2,1,0:T(8,128)(2,1)}, u32[]{:S(2)}) copy-start(bf16[32,512,128]{2,1,0:T(8,128)(2,1)} %param.13) | copy-start | bytes 12582916
  106.2 16.6 %copy-start.3 = (bf16[16384,128]{1,0:T(8,128)(2,1)}, bf16[16384,128]{1,0:T(8,128)(2,1)S(1)}, u32[]{:S(2)}) copy-start(bf16[16384,128]{1,0:T(8,128)(2,1)S(1)} %multiply_convert_fusion.2) | copy-start | bytes 12582916
  106.2 10.1 %collective-permute-start = (bf16[2,128]{1,0:T(2,128)(2,1)S(1)}, bf16[2,128]{1,0:T(2,128)(2,1)S(1)}, u32[]{:S(2)}, u32[]{:S(2)}) collective-permute-start(bf16[2,128]{1,0:T(2,128)(2,1)S(1)} %slice.68), channel_id=1, source_target_pairs={{0,8},{8,16},{16,24},{24,32},{32,40},{40,48},{48,56},{56,64},{64,7... | collective-permute-start | bytes 1544 | tf_op jit(solution)/shard_map/ppermute | solution.py:15
  122.8 3.0 copy-start.5
  122.8 5.0 copy-start.11
  125.9 1.9 copy-start.7
  140.1 61.4 %all-to-all-start.2 = ((bf16[32,512,128]{2,0,1:T(8,128)(2,1)}), bf16[32,512,128]{2,0,1:T(8,128)(2,1)}, u32[]{:S(2)}, u32[]{:S(2)}) async-start(bf16[32,512,128]{2,0,1:T(8,128)(2,1)} %copy.55), calls=%async_computation.2 | async-start | bytes 8388608 | tf_op jit(solution)/shard_map/all_to_all | solution.py:42
  201.5 61.0 %all-to-all-start = ((bf16[32,512,128]{2,0,1:T(8,128)(2,1)}), bf16[32,512,128]{2,0,1:T(8,128)(2,1)}, u32[]{:S(2)}, u32[]{:S(2)}) async-start(bf16[32,512,128]{2,0,1:T(8,128)(2,1)} %copy.45), calls=%async_computation | async-start | bytes 8388608 | tf_op jit(solution)/shard_map/all_to_all | solution.py:49
  262.5 61.0 %all-to-all-start.3 = ((bf16[512,32,128]{2,1,0:T(8,128)(2,1)}), bf16[512,32,128]{2,1,0:T(8,128)(2,1)}, u32[]{:S(2)}, u32[]{:S(2)}) async-start(bf16[512,32,128]{2,1,0:T(8,128)(2,1)} %copy.59), calls=%async_computation.3 | async-start | bytes 8388608 | tf_op jit(solution)/shard_map/all_to_all | solution.py:48
  267.6 4.1 copy-start.2
  271.7 12.6 %copy-start.4 = (bf16[16,32,32,128]{3,2,1,0:T(8,128)(2,1)}, bf16[16,32,32,128]{3,2,1,0:T(8,128)(2,1)S(1)}, u32[]{:S(2)}) copy-start(bf16[16,32,32,128]{3,2,1,0:T(8,128)(2,1)S(1)} %copy.47) | copy-start | bytes 12582916
  323.4 60.7 %all-to-all-start.1 = ((bf16[512,32,128]{2,1,0:T(8,128)(2,1)}), bf16[512,32,128]{2,1,0:T(8,128)(2,1)}, u32[]{:S(2)}, u32[]{:S(2)}) async-start(bf16[512,32,128]{2,1,0:T(8,128)(2,1)} %copy.50), calls=%async_computation.1 | async-start | bytes 8388608 | tf_op jit(solution)/shard_map/all_to_all | solution.py:56
  328.5 257.0 %all-reduce.7.cloned.1.call-start = ((), (), s32[]{:S(2)}) async-start(), calls=%async_computation.5 | async-start | bytes 4194304 | tf_op jit(solution)/shard_map/psum | solution.py:63
  384.2 5.5 copy-start.8
  387.8 1.9 copy-start.10
  427.0 3.3 copy-start.6
  430.3 5.9 collective-permute-start.2
  432.9 5.3 collective-permute-start.1
  501.8 86.8 %copy-start.1 = (bf16[512,512]{1,0:T(8,128)(2,1)S(1)}, bf16[512,512]{1,0:T(8,128)(2,1)}, u32[]{:S(2)}) copy-start(bf16[512,512]{1,0:T(8,128)(2,1)} %param.11) | copy-start | bytes 1572868
Sparse Core Ops, SparseCore 0:
  17.6 82.0 all-reduce.4
  435.0 150.5 all-reduce.6
where the time goes:
time: 606 us; the launch traced here: 596 us
  waiting for transfers between devices  240 us (40%)
  local copies, waits for them, and re-layouts  108 us (18%)
  other arithmetic  84.7 us (14%)
  blocking collectives  63.4 us (10%)
  matrix products  50.6 us (8%)
  starting transfers between devices  35.2 us (6%)
  between operations  14.5 us (2%)
    psum x1, waiting for transfers between devices, on_device(): squares = lax.psum(jnp.sum(flat_in * flat_in, axis=1), 'ch')  75.1 us
    all_to_all x1, waiting for transfers between devices, on_device(): lax.all_to_all(section_one, 'ctx', split_axis=1, concat_axis=0, tiled=True)  48.9 us
    psum x1, waiting for transfers between devices, on_device(): one_total, two_total = lax.psum((one_part, two_part), ('ctx', 'ch'))  39.4 us
    reduce_sum x1, other arithmetic, on_device(): gain_part = jnp.sum(grad_normed * hat, axis=0)  31.9 us
    psum x1, blocking collectives, on_device(): lax.psum(jnp.sum(scaled * hat, axis=1).astype(jnp.bfloat16), 'ch')  31.7 us
    psum x1, blocking collectives, on_device(): gain_total, taps_total = lax.psum((gain_part, tap_part), 'ctx')  31.7 us
    all_to_all x1, waiting for transfers between devices, on_device(): lax.all_to_all(section_two, 'ctx', split_axis=0, concat_axis=1, tiled=True)  31.2 us
    unnamed x33, local copies, waits for them, and re-layouts  30.4 us
  transfers between devices with their start and end apart: 9, of which 9 were waited for; matrix products, arithmetic and copies ran while one was open for 26% of the time, Pallas kernels for 0%

commit v1 on v0

--- a/solution.py
+++ b/solution.py
@@ -80,7 +80,9 @@
     gain_total, taps_total = lax.psum((gain_part, tap_part), "ctx")
     scaled = grad_normed * norm_gain
     row_mean = (
-        lax.psum(jnp.sum(scaled * hat, axis=1).astype(jnp.bfloat16), "ch").astype(jnp.float32)
+        jnp.sum(
+            lax.all_gather(jnp.sum(scaled * hat, axis=1).astype(jnp.bfloat16), "ch"), axis=0
+        ).astype(jnp.float32)
         / WIDTH
     )
     input_grad = (

time: 606 us -> 606 us (level)
    psum x1 -> x0, blocking collectives: 31.7 us -> none  [on_device(): lax.psum(jnp.sum(scaled * hat, axis=1).astype(jnp.bfloat16), 'ch')]
    all_gather x0 -> x1, blocking collectives: none -> 28.5 us  [on_device(): lax.all_gather(jnp.sum(scaled * hat, axis=1).astype(jnp.bfloat16), 'ch')]
where the time goes in v1:
time: 606 us; the launch traced here: 596 us
  waiting for transfers between devices  243 us (40%)
  local copies, waits for them, and re-layouts  108 us (18%)
  other arithmetic  84.9 us (14%)
  blocking collectives  59.3 us (10%)
  matrix products  50.6 us (8%)
  starting transfers between devices  35.2 us (6%)
  between operations  14.5 us (2%)
    psum x1, waiting for transfers between devices, on_device(): squares = lax.psum(jnp.sum(flat_in * flat_in, axis=1), 'ch')  75.1 us
    all_to_all x1, waiting for transfers between devices, on_device(): lax.all_to_all(section_one, 'ctx', split_axis=1, concat_axis=0, tiled=True)  48.9 us
    psum x1, waiting for transfers between devices, on_device(): one_total, two_total = lax.psum((one_part, two_part), ('ctx', 'ch'))  43.2 us
    reduce_sum x1, other arithmetic, on_device(): gain_part = jnp.sum(grad_normed * hat, axis=0)  31.9 us
    all_to_all x1, waiting for transfers between devices, on_device(): lax.all_to_all(section_two, 'ctx', split_axis=0, concat_axis=1, tiled=True)  31.2 us
    psum x1, blocking collectives, on_device(): gain_total, taps_total = lax.psum((gain_part, tap_part), 'ctx')  30.8 us
    unnamed x33, local copies, waits for them, and re-layouts  30.4 us
    all_to_all x1, waiting for transfers between devices, on_device(): lax.all_to_all(grad_section, 'ctx', split_axis=0, concat_axis=1, tiled=True)  29.1 us
  transfers between devices with their start and end apart: 9, of which 9 were waited for; matrix products, arithmetic and copies ran while one was open for 26% of the time, Pallas kernels for 0%

profile of v1, /device:TPU:1, one launch (start us, length us, event | category | flops | bytes accessed | tf_op | source)
XLA Modules:
  0.0 595.7 jit_solution(10027244180009093508)
XLA Ops:
  7.2 6.5 %copy.66 = bf16[32,512,128]{1,2,0:T(8,128)(2,1)} copy(bf16[32,512,128]{2,1,0:T(8,128)(2,1)} %param.7) | data formatting | bytes 8388608 | tf_op args[0]
  13.7 3.1 multiply_reduce_fusion.3
  17.5 7.1 %copy.67 = f32[32,512,128]{2,1,0:T(8,128)} copy(bf16[32,512,128]{1,2,0:T(8,128)(2,1)} %copy.66) | data formatting | bytes 12582912 | tf_op jit(solution)/shard_map/convert_element_type | solution.py:22
  24.6 75.1 %all-reduce.5.cloned.1.call-done = f32[16384]{0:T(1024)} async-done(((f32[16384]{0:T(1024)}), f32[16384]{0:T(1024)}) %all-reduce.5.cloned.1.call-update) | async-done | bytes 65552 | tf_op jit(solution)/shard_map/psum | solution.py:23
  100.7 5.5 multiply_convert_fusion.2
  106.2 9.4 %collective-permute-start = (bf16[2,128]{1,0:T(2,128)(2,1)S(1)}, bf16[2,128]{1,0:T(2,128)(2,1)S(1)}, u32[]{:S(2)}, u32[]{:S(2)}) collective-permute-start(bf16[2,128]{1,0:T(2,128)(2,1)S(1)} %slice.68), channel_id=1, source_target_pairs={{0,8},{8,16},{16,24},{24,32},{32,40},{40,48},{48,56},{56,64},{64,7... | collective-permute-start | bytes 1544 | tf_op jit(solution)/shard_map/ppermute | solution.py:15
  116.3 6.5 %fusion.10 = (bf16[16384,128]{1,0:T(8,128)(2,1)}, bf16[16384,128]{1,0:T(8,128)(2,1)S(1)}) fusion(bf16[32,512,128]{2,1,0:T(8,128)(2,1)S(1)} %copy-done.9, bf16[16384,128]{1,0:T(8,128)(2,1)S(1)} %multiply_convert_fusion.2, bf16[2,128]{1,0:T(2,128)(2,1)S(1)} %collective-permute-done, f32[128]{0:T(128)S(1)} %get-tuple-element.50, f32[128]{0:T(128)S(1)} %get-tuple-element.51, ...), kind=kLoop, calls=%fused_computation.29 | loop fusion | flops 44040192 | bytes 16779264 | tf_op jit(solution)/shard_map/convert_element_type | solution.py:41
  122.8 3.0 fusion.21
  125.9 1.9 copy-done.7
  127.8 4.4 convert_bitcast_fusion.3
  132.2 7.9 %copy.78 = bf16[32,512,128]{2,0,1:T(8,128)(2,1)} copy(bf16[32,512,128]{1,2,0:T(8,128)(2,1)} %convert_bitcast_fusion.3) | data formatting | bytes 8388608 | tf_op jit(solution)/shard_map/convert_element_type | solution.py:40
  140.1 5.6 all-to-all-start.2
  145.6 6.9 %copy.68 = bf16[32,512,128]{2,0,1:T(8,128)(2,1)} copy(bf16[32,512,128]{2,1,0:T(8,128)(2,1)} %bitcast.103) | data formatting | bytes 8388608 | tf_op jit(solution)/shard_map/reshape | solution.py:41
  152.6 48.9 %all-to-all-done.2 = bf16[32,512,128]{2,0,1:T(8,128)(2,1)} async-done(((bf16[32,512,128]{2,0,1:T(8,128)(2,1)}), bf16[32,512,128]{2,0,1:T(8,128)(2,1)}, u32[]{:S(2)}, u32[]{:S(2)}) %all-to-all-start.2) | async-done | bytes 4194336 | tf_op jit(solution)/shard_map/all_to_all | solution.py:42
  201.5 5.5 all-to-all-start
  207.0 7.6 %copy.72 = bf16[512,32,128]{0,2,1:T(8,128)(2,1)} copy(bf16[512,32,128]{2,1,0:T(8,128)(2,1)} %param.12) | data formatting | bytes 8388608 | tf_op args[5]
  214.5 3.8 copy.79
  219.5 4.2 copy.80
  223.8 9.9 %copy.81 = f32[512,32,128]{0,2,1:T(8,128)} copy(f32[512,32,128]{2,1,0:T(8,128)} %bitcast.102) | data formatting | bytes 16777216 | tf_op jit(solution)/shard_map/convert_element_type | solution.py:44
  233.7 8.9 %convert_bitcast_fusion.2 = bf16[512,32,128]{0,2,1:T(8,128)(2,1)} fusion(bf16[512,512]{1,0:T(8,128)(2,1)S(1)} %copy-done, f32[512,32,128]{0,2,1:T(8,128)} %copy.81, bf16[512,32,128]{0,2,1:T(8,128)(2,1)} %copy.72), kind=kOutput, calls=%fused_computation.66 | convolution fusion | flops 2155872256 | bytes 17301504 | tf_op jit(solution)/shard_map/ijc,ik->kjc/dot_general | solution.py:45
  242.6 7.9 %copy.82 = bf16[512,32,128]{2,1,0:T(8,128)(2,1)} copy(bf16[512,32,128]{0,2,1:T(8,128)(2,1)} %convert_bitcast_fusion.2) | data formatting | bytes 8388608 | tf_op jit(solution)/shard_map/convert_element_type | solution.py:47
  250.6 11.9 %all-to-all-done = bf16[32,512,128]{2,0,1:T(8,128)(2,1)} async-done(((bf16[32,512,128]{2,0,1:T(8,128)(2,1)}), bf16[32,512,128]{2,0,1:T(8,128)(2,1)}, u32[]{:S(2)}, u32[]{:S(2)}) %all-to-all-start) | async-done | bytes 4194336 | tf_op jit(solution)/shard_map/all_to_all | solution.py:49
  262.5 5.1 all-to-all-start.3
  267.6 4.1 copy.70
  271.7 12.6 %fusion.29 = (bf16[512,32,128]{0,2,1:T(8,128)(2,1)}, bf16[512,32,128]{0,2,1:T(8,128)(2,1)}) fusion(f32[512,32,128]{0,2,1:T(8,128)} %copy.81, bf16[512,32,128]{0,2,1:T(8,128)(2,1)S(1)} %copy-done.2, bf16[512,512]{1,0:T(8,128)(2,1)S(1)} %copy-done, bf16[512,32,128]{2,1,0:T(8,128)(2,1)S(1)} %bitcast.100), kind=kOutput, calls=%fused_computation.53 | convolution fusion | flops 2157969408 | bytes 25690112 | tf_op jit(solution)/shard_map/kjc,ik->ijc/dot_general | solution.py:50
  284.4 7.9 %copy.73 = bf16[512,32,128]{2,1,0:T(8,128)(2,1)} copy(bf16[512,32,128]{0,2,1:T(8,128)(2,1)} %get-tuple-element.48) | data formatting | bytes 8388608 | tf_op jit(solution)/shard_map/convert_element_type | solution.py:54
  292.3 31.2 %all-to-all-done.3 = bf16[512,32,128]{2,1,0:T(8,128)(2,1)} async-done(((bf16[512,32,128]{2,1,0:T(8,128)(2,1)}), bf16[512,32,128]{2,1,0:T(8,128)(2,1)}, u32[]{:S(2)}, u32[]{:S(2)}) %all-to-all-start.3) | async-done | bytes 4194336 | tf_op jit(solution)/shard_map/all_to_all | solution.py:48
  323.4 5.0 all-to-all-start.1
  328.5 7.8 %copy.87 = bf16[512,32,128]{2,1,0:T(8,128)(2,1)} copy(bf16[512,32,128]{0,2,1:T(8,128)(2,1)} %get-tuple-element.47) | data formatting | bytes 8388608
  336.4 11.0 %fusion.35 = f32[512,512]{1,0:T(8,128)} fusion(bf16[512,32,128]{2,1,0:T(8,128)(2,1)} %bitcast.101, f32[512,32,128]{0,2,1:T(8,128)} %copy.81, bf16[512,32,128]{0,2,1:T(8,128)(2,1)} %copy.72), kind=kOutput, calls=%fused_computation.73 | convolution fusion | flops 2153775104 | bytes 17825792 | tf_op jit(solution)/shard_map/ijc,kjc->ik/dot_general | solution.py:55
  347.4 3.4 convert_bitcast_fusion
  350.8 4.3 copy.83
  355.1 29.1 %all-to-all-done.1 = bf16[512,32,128]{2,1,0:T(8,128)(2,1)} async-done(((bf16[512,32,128]{2,1,0:T(8,128)(2,1)}), bf16[512,32,128]{2,1,0:T(8,128)(2,1)}, u32[]{:S(2)}, u32[]{:S(2)}) %all-to-all-start.1) | async-done | bytes 4194336 | tf_op jit(solution)/shard_map/all_to_all | solution.py:56
  384.2 3.6 copy.74
  387.8 1.9 copy-done.10
  389.7 3.3 convolution_bitcast_fusion.1
  393.1 10.3 %multiply_reduce_fusion = (f32[128]{0:T(128)S(1)}, f32[32,512,128]{1,2,0:T(8,128)}) fusion(f32[128]{0:T(128)S(1)} %copy-done.12, f32[32,512]{1,0:T(8,128)S(1)} %mul.250, bf16[32,512,128]{1,2,0:T(8,128)(2,1)} %copy.66, bf16[32,512,128]{2,1,0:T(8,128)(2,1)} %bitcast.108, bf16[512,512]{1,0:T(8,128)(2,1)S(1)} %copy-done.11), kind=kOutput, calls=%fused_computation.55 | convolution fusion | flops 2162163712 | bytes 17368064 | tf_op jit(solution)/shard_map/ikc,jk->ijc/dot_general | solution.py:59
  403.4 8.9 %copy.76 = f32[32,512,128]{2,1,0:T(8,128)} copy(f32[32,512,128]{1,2,0:T(8,128)} %get-tuple-element.56) | data formatting | bytes 16777216 | tf_op jit(solution)/shard_map/ikc,jk->ijc/transpose | solution.py:59
  413.0 14.0 %fusion.22 = (f32[128]{0:T(128)S(1)}, f32[128]{0:T(128)S(1)}, f32[128]{0:T(128)S(1)}, f32[128]{0:T(128)S(1)}, f32[128]{0:T(128)S(1)}, /*index=5*/f32[16384,128]{1,0:T(8,128)S(1)}) fusion(bf16[16384,128]{1,0:T(8,128)(2,1)} %copy-done.3, bf16[2,128]{1,0:T(2,128)(2,1)S(1)} %collective-permute-done, bf16[16384,128]{1,0:T(8,128)(2,1)} %copy-done.5, ...), kind=kLoop, calls=%fused_computation.41 | loop fusion | flops 60816768 | bytes 37753344 | tf_op jit(solution)/shard_map/reduce_sum | solution.py:77
  427.0 3.3 copy-done.6
  430.3 2.6 collective-permute-start.2
  436.2 1.9 collective-permute-done.1
  438.1 31.9 %multiply_reduce_fusion.1 = (f32[128]{0:T(128)S(1)}, bf16[16384]{0:T(1024)(128)(2,1)S(1)}, f32[16384,128]{1,0:T(8,128)}) fusion(f32[32,512,128]{2,1,0:T(8,128)} %copy.67, f32[16384]{0:T(1024)S(1)} %add_rsqrt_fusion, f32[128]{0:T(128)S(1)} %copy-done.12, f32[2,128]{1,0:T(2,128)S(1)} %collective-permute-done.2, f32[16384,128]{1,0:T(8,128)} %copy-done.6, ...), kind=kLoop, calls=%fused_computation.57 | loop fusion | flops 44023680 | bytes 33658880 | tf_op jit(solution)/shard_map/reduce_sum | solution.py:79
  470.1 28.5 %all-gather = bf16[131072]{0:T(1024)(128)(2,1)S(1)} all-gather(bf16[16384]{0:T(1024)(128)(2,1)S(1)} %get-tuple-element.31), channel_id=2, replica_groups=mesh['ctx'=16,'ch'=8] {'ch'}, dimensions={0}, use_global_device_ids=true | all-gather | bytes 294912 | tf_op jit(solution)/shard_map/all_gather | solution.py:84
  498.9 11.5 %multiply_convert_fusion.1 = bf16[16384,128]{1,0:T(8,128)(2,1)} fusion(f32[16384,128]{1,0:T(8,128)} %get-tuple-element.44, f32[32,512,128]{2,1,0:T(8,128)} %copy.67, f32[16384]{0:T(1024)S(1)} %convert_multiply_fusion.15, f32[128]{0:T(128)S(1)} %copy-done.12, f32[16384]{0:T(1024)S(1)} %add_rsqrt_fusion), kind=kLoop, calls=%fused_computation.58 | loop fusion | flops 12582912 | bytes 21103104 | tf_op jit(solution)/shard_map/convert_element_type | solution.py:90
  510.4 30.8 %all-reduce.1 = (f32[128]{0:T(128)S(1)}, f32[2,3,128]{2,1,0:T(4,128)S(1)}) all-reduce(f32[128]{0:T(128)S(1)} %get-tuple-element.30, f32[2,3,128]{2,1,0:T(4,128)S(1)} %pad_maximum_fusion.3), channel_id=1, replica_groups=mesh['ctx'=16,'ch'=8] {'ctx'}, use_global_device_ids=true, to_apply=%region_7.0 | all-reduce | flops 896 | bytes 7168 | tf_op jit(solution)/shard_map/psum | solution.py:80
  542.4 43.2 %all-reduce.7.cloned.1.call-done = (f32[512,512]{1,0:T(8,128)}, f32[512,512]{1,0:T(8,128)}) async-done(((f32[512,512]{1,0:T(8,128)}, f32[512,512]{1,0:T(8,128)}), (f32[512,512]{1,0:T(8,128)}, f32[512,512]{1,0:T(8,128)})) %all-reduce.7.cloned.1.call-update) | async-done | bytes 2097168 | tf_op jit(solution)/shard_map/psum | solution.py:63
  585.5 3.1 broadcast_multiply_fusion
  (48 shorter events, 9.1 us)
Async XLA Ops:
  7.2 226.5 %copy-start = (bf16[512,512]{1,0:T(8,128)(2,1)S(1)}, bf16[512,512]{1,0:T(8,128)(2,1)}, u32[]{:S(2)}) copy-start(bf16[512,512]{1,0:T(8,128)(2,1)} %param.11) | copy-start | bytes 1572868
  7.2 92.5 %all-reduce.5.cloned.1.call-start = ((), (), s32[]{:S(2)}) async-start(), calls=%async_computation.4 | async-start | bytes 131072 | tf_op jit(solution)/shard_map/psum | solution.py:23
  13.7 87.0 %copy-start.12 = (f32[128]{0:T(128)S(1)}, f32[128]{0:T(128)}, u32[]{:S(2)}) copy-start(f32[128]{0:T(128)} %param.8) | copy-start | bytes 1540
  24.6 91.1 %copy-start.13 = (f32[2,3,128]{2,0,1:T(2,128)S(1)}, f32[2,3,128]{2,0,1:T(2,128)}, u32[]{:S(2)}) copy-start(f32[2,3,128]{2,0,1:T(2,128)} %param.9) | copy-start | bytes 9220
  99.7 16.6 %copy-start.9 = (bf16[32,512,128]{2,1,0:T(8,128)(2,1)S(1)}, bf16[32,512,128]{2,1,0:T(8,128)(2,1)}, u32[]{:S(2)}) copy-start(bf16[32,512,128]{2,1,0:T(8,128)(2,1)} %param.13) | copy-start | bytes 12582916
  106.2 16.6 %copy-start.3 = (bf16[16384,128]{1,0:T(8,128)(2,1)}, bf16[16384,128]{1,0:T(8,128)(2,1)S(1)}, u32[]{:S(2)}) copy-start(bf16[16384,128]{1,0:T(8,128)(2,1)S(1)} %multiply_convert_fusion.2) | copy-start | bytes 12582916
  106.2 10.1 %collective-permute-start = (bf16[2,128]{1,0:T(2,128)(2,1)S(1)}, bf16[2,128]{1,0:T(2,128)(2,1)S(1)}, u32[]{:S(2)}, u32[]{:S(2)}) collective-permute-start(bf16[2,128]{1,0:T(2,128)(2,1)S(1)} %slice.68), channel_id=1, source_target_pairs={{0,8},{8,16},{16,24},{24,32},{32,40},{40,48},{48,56},{56,64},{64,7... | collective-permute-start | bytes 1544 | tf_op jit(solution)/shard_map/ppermute | solution.py:15
  122.8 3.0 copy-start.5
  122.8 5.0 copy-start.11
  125.9 1.9 copy-start.7
  140.1 61.4 %all-to-all-start.2 = ((bf16[32,512,128]{2,0,1:T(8,128)(2,1)}), bf16[32,512,128]{2,0,1:T(8,128)(2,1)}, u32[]{:S(2)}, u32[]{:S(2)}) async-start(bf16[32,512,128]{2,0,1:T(8,128)(2,1)} %copy.78), calls=%async_computation.2 | async-start | bytes 8388608 | tf_op jit(solution)/shard_map/all_to_all | solution.py:42
  201.5 61.0 %all-to-all-start = ((bf16[32,512,128]{2,0,1:T(8,128)(2,1)}), bf16[32,512,128]{2,0,1:T(8,128)(2,1)}, u32[]{:S(2)}, u32[]{:S(2)}) async-start(bf16[32,512,128]{2,0,1:T(8,128)(2,1)} %copy.68), calls=%async_computation | async-start | bytes 8388608 | tf_op jit(solution)/shard_map/all_to_all | solution.py:49
  262.5 61.0 %all-to-all-start.3 = ((bf16[512,32,128]{2,1,0:T(8,128)(2,1)}), bf16[512,32,128]{2,1,0:T(8,128)(2,1)}, u32[]{:S(2)}, u32[]{:S(2)}) async-start(bf16[512,32,128]{2,1,0:T(8,128)(2,1)} %copy.82), calls=%async_computation.3 | async-start | bytes 8388608 | tf_op jit(solution)/shard_map/all_to_all | solution.py:48
  267.6 4.1 copy-start.2
  271.7 12.6 %copy-start.4 = (bf16[16,32,32,128]{3,2,1,0:T(8,128)(2,1)}, bf16[16,32,32,128]{3,2,1,0:T(8,128)(2,1)S(1)}, u32[]{:S(2)}) copy-start(bf16[16,32,32,128]{3,2,1,0:T(8,128)(2,1)S(1)} %copy.70) | copy-start | bytes 12582916
  323.4 60.7 %all-to-all-start.1 = ((bf16[512,32,128]{2,1,0:T(8,128)(2,1)}), bf16[512,32,128]{2,1,0:T(8,128)(2,1)}, u32[]{:S(2)}, u32[]{:S(2)}) async-start(bf16[512,32,128]{2,1,0:T(8,128)(2,1)} %copy.73), calls=%async_computation.1 | async-start | bytes 8388608 | tf_op jit(solution)/shard_map/all_to_all | solution.py:56
  328.5 257.0 %all-reduce.7.cloned.1.call-start = ((), (), s32[]{:S(2)}) async-start(), calls=%async_computation.5 | async-start | bytes 4194304 | tf_op jit(solution)/shard_map/psum | solution.py:63
  384.2 5.5 copy-start.8
  387.8 1.9 copy-start.10
  427.0 3.3 copy-start.6
  430.3 5.9 collective-permute-start.2
  432.9 5.3 collective-permute-start.1
  498.9 89.7 %copy-start.1 = (bf16[512,512]{1,0:T(8,128)(2,1)S(1)}, bf16[512,512]{1,0:T(8,128)(2,1)}, u32[]{:S(2)}) copy-start(bf16[512,512]{1,0:T(8,128)(2,1)} %param.11) | copy-start | bytes 1572868
Sparse Core Ops, SparseCore 0:
  17.6 82.0 all-reduce.4
  435.0 150.5 all-reduce.6
